TPU v7x, 32 devices: a whole 2x2x4 slice. The times are simulated.
32 devices in a mesh: groups: 2 (over y), events: 8 (over z, x), heads: 2 (over core).
Axes of the slice: x: 2, y: 2, z: 4, core: 2. Of those that a mesh axis runs over, the one named last changes fastest.
Arguments:
- inputs: bfloat16 [256, 1024], P(('groups', 'events')), parts along dimension 0, may hold values from -6 to 6
- cand_user: int32 [256], P('groups'), parts along dimension 0, may hold values from 0 to 3, as said below
- event_user: int32 [8192], P(('groups', 'events')), parts along dimension 0, may hold values from 0 to 3, as said below
- event_count: int32 [16], P(('groups', 'events')), parts along dimension 0, may hold values from 128 to 512, as said below
- w_qu: bfloat16 [1024, 2, 1024], P(None, None, 'heads'), may hold values from -0.1875 to 0.1875
- keys: bfloat16 [8192, 1024], P(('groups', 'events'), 'heads'), parts along dimension 0, may hold values from -6 to 6
- values: bfloat16 [8192, 1024], P(('groups', 'events'), 'heads'), parts along dimension 0, may hold values from -6 to 6
- gain: float32 [1024], P('heads'), may hold values from 0.1 to 1.9
- w_out: bfloat16 [1024, 1024], P('heads'), may hold values from -0.1875 to 0.1875
Outputs:
- scored: bfloat16 [256, 1024], P(('groups', 'events')), parts along dimension 0
There are 2 independent parts, one for each index of `groups`. A program takes and returns all parts, laid end to end along the dimension named above; an argument that names none is the same for every part. Nothing has to cross between parts.
Inputs may be any that keep to these rules, and one draw needn't show every extreme that they name: `event_count`: each cache shard's filled slots come first; some shard is full and some holds 128. `event_user`: Users' events are consecutive and in increasing user order over the whole cache; every user has 1 to 2047 events, and some user has exactly 2047. `cand_user`: every candidate belongs to a user that has at least one filled slot somewhere in the cache.
All inputs are finite; a program needn't handle non-finite values.
Results may differ from a plain program's by a relative error of at most 0.0075.
Values may be sent and summed in bfloat16 or wider, within the bound.
No kernel may reach another device: no remote copies, remote signals or barrier semaphores. Data moves between devices by JAX's collectives and lax.ppermute only.
A program may use at most 64 MiB of HBM per device.

v0:
```python
import math

import jax
import jax.numpy as jnp
from jax import lax
from jax.sharding import PartitionSpec as P

DH = 128
HD = 1024


epsilon = 1e-05


def shards(inputs, cand_user, event_user, event_count, w_qu, keys, values, gain, w_out):
    row_count = inputs.shape[0]
    feat_width = inputs.shape[1]
    local_width = w_qu.shape[2]
    heads_here = local_width // DH
    slot_total = keys.shape[0]
    score_scale = 1.0 / math.sqrt(DH)
    packed_weight = w_qu.reshape(feat_width, 2 * local_width)
    query_weight = packed_weight[:, :local_width]
    gate_weight = packed_weight[:, local_width:]
    gate_values = jax.nn.silu(
        jnp.dot(inputs, gate_weight, preferred_element_type=jnp.float32)
    ).astype(jnp.bfloat16)
    gathered_rows = lax.all_gather(inputs, "events", axis=0, tiled=True)
    queries = jax.nn.silu(
        jnp.dot(gathered_rows, query_weight, preferred_element_type=jnp.float32)
    ).astype(jnp.bfloat16)
    slot_index = jnp.arange(slot_total, dtype=jnp.int32)
    slot_valid = slot_index < event_count[0]
    key_heads = keys.reshape(slot_total, heads_here, DH)
    value_heads = values.reshape(slot_total, heads_here, DH)

    def attend_rows(query_rows, row_users):
        rows_here = query_rows.shape[0]
        query_block = query_rows.reshape(rows_here, heads_here, DH)
        user_match = ((row_users[:, None] == event_user[None, :]) & slot_valid[None, :]).astype(
            jnp.float32
        )
        scores = (
            jnp.einsum("chd,ehd->hce", query_block, key_heads, preferred_element_type=jnp.float32)
            * score_scale
        )
        attn_weights = (jax.nn.silu(scores) * user_match[None]).astype(jnp.bfloat16)
        partial_out = jnp.einsum(
            "hce,ehd->chd", attn_weights, value_heads, preferred_element_type=jnp.float32
        )
        return partial_out.reshape(rows_here, local_width)

    block_rows = math.gcd(row_count * lax.axis_size("events"), 512)
    block_count = row_count * lax.axis_size("events") // block_rows

    def compute_block(which_block):
        block_start = which_block * block_rows
        query_rows = lax.dynamic_slice_in_dim(queries, block_start, block_rows, 0)
        block_users = lax.dynamic_slice_in_dim(cand_user, block_start, block_rows, 0)
        return attend_rows(query_rows, block_users)

    stacked = lax.map(compute_block, jnp.arange(block_count, dtype=jnp.int32))
    attended = lax.psum_scatter(
        stacked.reshape(row_count * lax.axis_size("events"), local_width),
        "events",
        scatter_dimension=0,
        tiled=True,
    )
    first_moment = jnp.sum(attended, axis=1)
    second_moment = jnp.sum(attended * attended, axis=1)
    total_first, total_second = lax.psum((first_moment, second_moment), "heads")
    average = total_first / HD
    variance = total_second / HD - average * average
    normed = (attended - average[:, None]) * lax.rsqrt(variance + epsilon)[:, None] * gain
    gated = (normed * gate_values.astype(jnp.float32)).astype(jnp.bfloat16)
    projected = jnp.dot(gated, w_out, preferred_element_type=jnp.float32)
    summed_heads = lax.psum(projected, "heads")
    return (inputs.astype(jnp.float32) + summed_heads).astype(jnp.bfloat16)


def solution(mesh):
    placed = (
        P(("groups", "events"), None),
        P("groups"),
        P(("groups", "events")),
        P(("groups", "events")),
        P(None, None, "heads"),
        P(("groups", "events"), "heads"),
        P(("groups", "events"), "heads"),
        P("heads"),
        P("heads", None),
    )
    return jax.shard_map(
        shards, mesh=mesh, in_specs=placed, out_specs=P(("groups", "events"), None), check_vma=False
    )
```

profile of v0, /device:TPU:0, one launch (start us, length us, event | category | flops | bytes accessed | tf_op | source)
XLA Modules:
  0.0 143.9 jit_solution(11439747766623471906)
XLA Ops:
  6.5 0.0 copy-start
  6.5 0.0 reduce-scatter.2.cloned.1.call-start
  7.3 32.8 %all_gather.3 = bf16[128,1024]{1,0:T(8,128)(2,1)S(1)} all-gather(bf16[16,1024]{1,0:T(8,128)(2,1)} %param.9), channel_id=1, replica_groups=mesh['groups'=2,'events'=8,'heads'=2] {'events'}, dimensions={0}, use_global_device_ids=true | all-gather | bytes 294912 | tf_op jit(solution)/shard_map/all_gather | solution.py:28
  40.1 2.0 %copy.14 = bf16[512,512]{0,1:T(8,128)(2,1)} copy(bf16[512,512]{1,0:T(8,128)(2,1)} %param.15) | data formatting | bytes 1048576 | tf_op jit(solution)/shard_map/reshape | solution.py:35
  42.1 2.2 %copy.17 = bf16[128,8,2,512]{3,1,2,0:T(8,128)(2,1)S(1)} copy(bf16[128,8,2,512]{3,2,1,0:T(2,128)(2,1)} %bitcast.29) | data formatting | bytes 4194304
  44.3 0.0 copy-start.2
  44.3 0.0 copy-start.4
  44.3 1.0 fusion.14
  45.3 0.0 copy-done.2
  45.3 0.0 copy-done.4
  45.3 0.1 and_convert_fusion
  45.4 0.0 copy-start.1
  45.4 0.0 copy-start.3
  45.4 2.6 %fusion.4 = f32[4,128,128]{1,2,0:T(8,128)} fusion(bf16[512,4,128]{0,2,1:T(8,128)(2,1)} %bitcast.30, f32[128,512]{1,0:T(8,128)S(1)} %and_convert_fusion, bf16[16,4,8,128]{3,2,1,0:T(8,128)(2,1)} %fusion.14, bf16[512,512]{1,0:T(8,128)(2,1)} %param.14), kind=kOutput, calls=%fused_computation.6 | convolution fusion | flops 136052736 | bytes 1703936 | tf_op jit(solution)/shard_map/while/body/eval_jaxpr/hce,ehd->chd/dot_general | solution.py:48
  48.1 1.8 %copy.13 = f32[128,512]{1,0:T(8,128)} copy(f32[128,512]{0,1:T(8,128)} %bitcast.31) | data formatting | bytes 524288 | tf_op jit(solution)/shard_map/reshape | solution.py:64
  49.9 0.0 reduce-scatter.2.cloned.1.call-update
  49.9 0.0 all-reduce.3.cloned.1.call-start
  49.9 63.5 %reduce-scatter.2.cloned.1.call-done = f32[16,512]{1,0:T(8,128)} async-done(((f32[128,512]{1,0:T(8,128)}), f32[16,512]{1,0:T(8,128)}) %reduce-scatter.2.cloned.1.call-update) | async-done | bytes 32784 | tf_op jit(solution)/shard_map/reduce_scatter | solution.py:63
  113.5 0.9 fusion.38
  114.3 2.5 %all-reduce = (f32[16]{0:T(128)S(1)}, f32[16]{0:T(128)S(1)}) all-reduce(f32[16]{0:T(128)S(1)} %get-tuple-element.20, f32[16]{0:T(128)S(1)} %get-tuple-element.19), channel_id=1, replica_groups=mesh['groups'=2,'events'=8,'heads'=2] {'heads'}, use_global_device_ids=true, to_apply=%region_4.5 | all-reduce | flops 32 | bytes 256 | tf_op jit(solution)/shard_map/psum | solution.py:71
  116.8 0.0 copy-done
  116.8 0.0 copy-done.1
  116.8 0.0 copy-done.3
  116.8 1.9 %fusion.26 = f32[16,1024]{1,0:T(8,128)} fusion(bf16[512,1024]{1,0:T(8,128)(2,1)S(1)} %copy-done, bf16[16,1024]{1,0:T(8,128)(2,1)S(1)} %copy-done.1, bf16[1024,1024]{1,0:T(8,128)(2,1)S(1)} %bitcast.28, f32[16,512]{1,0:T(8,128)} %reduce-scatter.2.cloned.1.call-done, f32[512]{0:T(512)S(1)} %copy-done.3, f32[16]{0:T(128)S(1)} %get-tuple-element.32, ...), kind=kOutput, calls=%fused_computation.20 | convolution fusion | flops 33644544 | bytes 2231296 | tf_op jit(solution)/shard_map/dot_general | solution.py:76
  118.7 0.0 all-reduce.3.cloned.1.call-update
  118.7 16.9 %all-reduce.3.cloned.1.call-done = f32[16,1024]{1,0:T(8,128)} async-done(((f32[16,1024]{1,0:T(8,128)}), f32[16,1024]{1,0:T(8,128)}) %all-reduce.3.cloned.1.call-update) | async-done | bytes 65552 | tf_op jit(solution)/shard_map/psum | solution.py:77
  135.6 1.5 %add_convert_fusion = bf16[16,1024]{1,0:T(8,128)(2,1)} fusion(f32[16,1024]{1,0:T(8,128)} %all-reduce.3.cloned.1.call-done, bf16[16,1024]{1,0:T(8,128)(2,1)S(1)} %copy-done.1), kind=kLoop, calls=%fused_computation.17 | loop fusion | flops 49152 | bytes 131072 | tf_op jit(solution)/shard_map/convert_element_type | solution.py:78
  (2 shorter events, 0.0 us)
Async XLA Ops:
  6.5 110.3 %copy-start = (bf16[512,1024]{1,0:T(8,128)(2,1)S(1)}, bf16[512,1024]{1,0:T(8,128)(2,1)}, u32[]{:S(2)}) copy-start(bf16[512,1024]{1,0:T(8,128)(2,1)} %param.17) | copy-start | bytes 3145732
  6.5 106.9 %reduce-scatter.2.cloned.1.call-start = ((), (), s32[]{:S(2)}) async-start(), calls=%async_computation.1 | async-start | bytes 294912 | tf_op jit(solution)/shard_map/reduce_scatter | solution.py:63
  44.3 1.0 copy-start.2
  44.3 1.0 copy-start.4
  45.4 71.4 %copy-start.1 = (bf16[16,1024]{1,0:T(8,128)(2,1)S(1)}, bf16[16,1024]{1,0:T(8,128)(2,1)}, u32[]{:S(2)}) copy-start(bf16[16,1024]{1,0:T(8,128)(2,1)} %param.9) | copy-start | bytes 98308
  45.4 71.4 %copy-start.3 = (f32[512]{0:T(512)S(1)}, f32[512]{0:T(512)}, u32[]{:S(2)}) copy-start(f32[512]{0:T(512)} %param.16) | copy-start | bytes 6148
  49.9 85.7 %all-reduce.3.cloned.1.call-start = ((), (), s32[]{:S(2)}) async-start(), calls=%async_computation.2 | async-start | bytes 131072 | tf_op jit(solution)/shard_map/psum | solution.py:77
Sparse Core Ops, SparseCore 0:
  50.0 63.4 reduce-scatter.1
  118.8 16.7 all-reduce.2
where the time goes:
time: 144 us
  waiting for transfers between devices  80.5 us (56%)
  blocking collectives  35.2 us (24%)
  between operations  14.2 us (10%)
  local copies, waits for them, and re-layouts  6 us (4%)
  matrix products  5.52 us (4%)
  other arithmetic  2.45 us (2%)
    reduce_scatter x1, waiting for transfers between devices, shards(): lax.psum_scatter(stacked.reshape(row_count * lax.axis_size('events'), loc...  63.5 us
    all_gather x1, blocking collectives, shards(): gathered_rows = lax.all_gather(inputs, 'events', axis=0, tiled=True)  32.8 us
    psum x1, waiting for transfers between devices, shards(): summed_heads = lax.psum(projected, 'heads')  16.9 us
  transfers between devices with their start and end apart: 2, of which 2 were waited for; matrix products, arithmetic and copies ran while one was open for 0% of the time, Pallas kernels for 0%

commit v1 on v0

v1 whole, which is shorter than its diff:
```python
import math

import jax
import jax.numpy as jnp
from jax import lax
from jax.sharding import PartitionSpec as P

DH = 128
HD = 1024


epsilon = 1e-05


def partner_sum(x):
    n = lax.axis_size("heads")
    other = lax.ppermute(x, "heads", [(i, (i + 1) % n) for i in range(n)])
    return x + other


def shards(inputs, cand_user, event_user, event_count, w_qu, keys, values, gain, w_out):
    row_count = inputs.shape[0]
    feat_width = inputs.shape[1]
    local_width = w_qu.shape[2]
    heads_here = local_width // DH
    slot_total = keys.shape[0]
    n_ev = lax.axis_size("events")
    score_scale = 1.0 / math.sqrt(DH)

    packed_weight = w_qu.reshape(feat_width, 2 * local_width)
    proj = jax.nn.silu(jnp.dot(inputs, packed_weight, preferred_element_type=jnp.float32))
    query_local = proj[:, :local_width].astype(jnp.bfloat16)
    gate_values = proj[:, local_width:].astype(jnp.bfloat16)

    spread = jnp.broadcast_to(query_local[None], (n_ev, row_count, local_width))
    queries = lax.all_to_all(spread, "events", 0, 0, tiled=False).reshape(n_ev * row_count, local_width)

    slot_index = jnp.arange(slot_total, dtype=jnp.int32)
    slot_valid = slot_index < event_count[0]
    key_heads = keys.reshape(slot_total, heads_here, DH)
    value_heads = values.reshape(slot_total, heads_here, DH)
    all_rows = queries.shape[0]
    query_block = queries.reshape(all_rows, heads_here, DH)
    user_match = ((cand_user[:, None] == event_user[None, :]) & slot_valid[None, :]).astype(jnp.float32)
    scores = (
        jnp.einsum("chd,ehd->hce", query_block, key_heads, preferred_element_type=jnp.float32)
        * score_scale
    )
    attn_weights = (jax.nn.silu(scores) * user_match[None]).astype(jnp.bfloat16)
    partial_out = jnp.einsum(
        "hce,ehd->chd", attn_weights, value_heads, preferred_element_type=jnp.float32
    ).reshape(n_ev, row_count, local_width)

    pieces = lax.all_to_all(partial_out, "events", 0, 0, tiled=False)
    attended = jnp.sum(pieces, axis=0)

    moments = jnp.stack([jnp.sum(attended, axis=1), jnp.sum(attended * attended, axis=1)])
    moments = partner_sum(moments)
    average = moments[0] / HD
    variance = moments[1] / HD - average * average
    normed = (attended - average[:, None]) * lax.rsqrt(variance + epsilon)[:, None] * gain
    gated = (normed * gate_values.astype(jnp.float32)).astype(jnp.bfloat16)
    projected = jnp.dot(gated, w_out, preferred_element_type=jnp.float32)
    summed_heads = partner_sum(projected)
    return (inputs.astype(jnp.float32) + summed_heads).astype(jnp.bfloat16)


def solution(mesh):
    placed = (
        P(("groups", "events"), None),
        P("groups"),
        P(("groups", "events")),
        P(("groups", "events")),
        P(None, None, "heads"),
        P(("groups", "events"), "heads"),
        P(("groups", "events"), "heads"),
        P("heads"),
        P("heads", None),
    )
    return jax.shard_map(
        shards, mesh=mesh, in_specs=placed, out_specs=P(("groups", "events"), None), check_vma=False
    )
```

time: 144 us -> 33.7 us (0.23)
  waiting for transfers between devices: 80.5 us -> 8.79 us
  blocking collectives: 35.2 us -> 10.6 us
  between operations: 14.2 us -> 0.83 us
  starting transfers between devices: 0.04 us -> 7.52 us
  matrix products: 5.52 us -> 1.34 us
  local copies, waits for them, and re-layouts: 6 us -> 3.26 us
    reduce_scatter x1 -> x0, waiting for transfers between devices: 63.5 us -> none  [shards(): lax.psum_scatter(stacked.reshape(row_count * lax.axis_size('events'), loc...]
    all_gather x1 -> x0, blocking collectives: 32.8 us -> none  [shards(): gathered_rows = lax.all_gather(inputs, 'events', axis=0, tiled=True)]
    psum x1 -> x0, waiting for transfers between devices: 16.9 us -> none  [shards(): summed_heads = lax.psum(projected, 'heads')]
    all_to_all x0 -> x1, blocking collectives: none -> 10.6 us  [shards(): pieces = lax.all_to_all(partial_out, 'events', 0, 0, tiled=False)]
    all_to_all x0 -> x1, starting transfers between devices: none -> 7.28 us  [shards(): lax.all_to_all(spread, 'events', 0, 0, tiled=False)]
    all_to_all x0 -> x1, waiting for transfers between devices: none -> 6.55 us  [shards(): lax.all_to_all(spread, 'events', 0, 0, tiled=False)]
    reshape x2 -> x1, local copies, waits for them, and re-layouts: 3.82 us -> 0.11 us  [shards(): partial_out = jnp.einsum('hce,ehd->chd', attn_weights, value_heads, prefe...]
    dot_general x2, matrix products: 3.65 us -> 1.05 us  [the longest x1 0.65 us: shards(): jnp.einsum('hce,ehd->chd', attn_weights, value_heads, preferred_element_t...]
  transfers between devices with their start and end apart: 2 -> 3, of which waited for: 2 -> 3; matrix products, arithmetic and copies ran while one was open for 0% -> 0% of each run, Pallas kernels for 0% -> 0%
where the time goes in v1:
time: 33.7 us; the launch traced here: 33.4 us
  blocking collectives  10.6 us (31%)
  waiting for transfers between devices  8.79 us (26%)
  starting transfers between devices  7.52 us (22%)
  local copies, waits for them, and re-layouts  3.26 us (10%)
  matrix products  1.34 us (4%)
  other arithmetic  1.03 us (3%)
  between operations  0.83 us (2%)
    all_to_all x1, blocking collectives, shards(): pieces = lax.all_to_all(partial_out, 'events', 0, 0, tiled=False)  10.6 us
    all_to_all x1, starting transfers between devices, shards(): lax.all_to_all(spread, 'events', 0, 0, tiled=False)  7.28 us
    all_to_all x1, waiting for transfers between devices, shards(): lax.all_to_all(spread, 'events', 0, 0, tiled=False)  6.55 us
    unnamed x15, local copies, waits for them, and re-layouts  2.29 us
    ppermute x2, waiting for transfers between devices, partner_sum(): other = lax.ppermute(x, 'heads', [(i, (i + 1) % n) for i in range(n)])  2.24 us
  transfers between devices with their start and end apart: 3, of which 3 were waited for; matrix products, arithmetic and copies ran while one was open for 0% of the time, Pallas kernels for 0%

profile of v1, /device:TPU:0, one launch (start us, length us, event | category | flops | bytes accessed | tf_op | source)
XLA Modules:
  0.0 33.4 jit_solution(4165785390494035630)
XLA Ops:
  0.0 0.0 copy-start
  0.0 0.0 copy-start.1
  0.0 2.3 %copy.18 = bf16[128,8,2,512]{3,1,2,0:T(8,128)(2,1)S(1)} copy(bf16[128,8,2,512]{3,2,1,0:T(2,128)(2,1)} %bitcast.38) | data formatting | bytes 4194304
  2.3 0.0 copy-start.2
  2.3 0.0 copy-start.4
  2.3 0.0 copy-start.5
  2.3 0.0 copy-start.6
  2.3 0.0 copy-done.1
  2.3 0.4 %multiply_convert_fusion.1 = bf16[16,1024]{1,0:T(8,128)(2,1)S(1)} fusion(bf16[16,1024]{1,0:T(8,128)(2,1)S(1)} %copy-done.1, bf16[1024,1024]{1,0:T(8,128)(2,1)S(1)} %bitcast.37), kind=kOutput, calls=%fused_computation.13 | convolution fusion | flops 33636352 | bytes 2162688 | tf_op jit(solution)/shard_map/dot_general | solution.py:31
  2.8 0.7 %broadcast_in_dim.2 = bf16[8,16,512]{2,1,0:T(8,128)(2,1)} broadcast(bf16[16,512]{1,0:T(8,128)(2,1)S(1)} %slice.18), dimensions={1,2} | broadcast | bytes 147456 | tf_op jit(solution)/shard_map/broadcast_in_dim | solution.py:35
  3.4 7.3 %all-to-all-start = ((bf16[8,16,512]{2,1,0:T(8,128)(2,1)}), bf16[8,16,512]{2,1,0:T(8,128)(2,1)S(1)}, u32[]{:S(2)}, u32[]{:S(2)}) async-start(bf16[8,16,512]{2,1,0:T(8,128)(2,1)} %broadcast_in_dim.2), calls=%async_computation | async-start | bytes 262144 | tf_op jit(solution)/shard_map/all_to_all | solution.py:36
  11.3 0.0 copy-done.2
  11.4 0.0 copy-done.4
  11.4 0.1 and_convert_fusion
  11.5 6.5 %all-to-all-done = bf16[8,16,512]{2,1,0:T(8,128)(2,1)S(1)} async-done(((bf16[8,16,512]{2,1,0:T(8,128)(2,1)}), bf16[8,16,512]{2,1,0:T(8,128)(2,1)S(1)}, u32[]{:S(2)}, u32[]{:S(2)}) %all-to-all-start) | async-done | bytes 131104 | tf_op jit(solution)/shard_map/all_to_all | solution.py:36
  18.1 0.0 copy-done.5
  18.1 0.0 copy-done.6
  18.1 0.0 copy-start.3
  18.1 0.6 %convolution_bitcast_fusion = f32[128,4,128]{2,0,1:T(8,128)S(1)} fusion(f32[128,512]{1,0:T(8,128)S(1)} %and_convert_fusion, bf16[128,4,128]{2,1,0:T(4,128)(2,1)S(1)} %reshape_reshape.3, bf16[512,512]{1,0:T(8,128)(2,1)S(1)} %copy-done.5, bf16[512,512]{1,0:T(8,128)(2,1)S(1)} %copy-done.6), kind=kOutput, calls=%fused_computation.1 | convolution fusion | flops 136052736 | bytes 1703936 | tf_op jit(solution)/shard_map/hce,ehd->chd/dot_general | solution.py:50
  18.7 0.2 copy.15
  18.9 0.1 reshape.85
  19.0 10.6 %all_to_all.10 = f32[8,16,512]{2,1,0:T(8,128)S(1)} all-to-all(f32[8,16,512]{2,1,0:T(8,128)S(1)} %reshape.85), channel_id=1, replica_groups=mesh['groups'=2,'events'=8,'heads'=2] {'events'}, dimensions={0} | all-to-all | bytes 524288 | tf_op jit(solution)/shard_map/all_to_all | solution.py:54
  29.7 0.1 fusion.21
  29.8 0.1 multiply_reduce_fusion
  30.0 0.1 collective-permute-start
  30.0 1.1 %collective-permute-done = f32[2,16]{1,0:T(2,128)S(1)} collective-permute-done((f32[2,16]{1,0:T(2,128)S(1)}, f32[2,16]{1,0:T(2,128)S(1)}, u32[]{:S(2)}, u32[]{:S(2)}) %collective-permute-start) | collective-permute-done | bytes 160 | tf_op jit(solution)/shard_map/ppermute | solution.py:17
  31.2 0.0 copy-done
  31.2 0.0 copy-done.3
  31.2 0.3 fusion.11
  31.5 0.2 collective-permute-start.1
  31.7 1.1 %collective-permute-done.1 = f32[16,1024]{1,0:T(8,128)S(1)} collective-permute-done((f32[16,1024]{1,0:T(8,128)S(1)}, f32[16,1024]{1,0:T(8,128)S(1)}, u32[]{:S(2)}, u32[]{:S(2)}) %collective-permute-start.1) | collective-permute-done | bytes 65568 | tf_op jit(solution)/shard_map/ppermute | solution.py:17
  32.8 0.6 %add_convert_fusion = bf16[16,1024]{1,0:T(8,128)(2,1)} fusion(f32[16,1024]{1,0:T(8,128)S(1)} %fusion.11, f32[16,1024]{1,0:T(8,128)S(1)} %collective-permute-done.1, bf16[16,1024]{1,0:T(8,128)(2,1)S(1)} %copy-done.1), kind=kLoop, calls=%fused_computation.12 | loop fusion | flops 65536 | bytes 196608 | tf_op jit(solution)/shard_map/convert_element_type | solution.py:65
  (7 shorter events, 0.1 us)
Async XLA Ops:
  0.0 31.2 %copy-start = (bf16[512,1024]{1,0:T(8,128)(2,1)S(1)}, bf16[512,1024]{1,0:T(8,128)(2,1)}, u32[]{:S(2)}) copy-start(bf16[512,1024]{1,0:T(8,128)(2,1)} %param.17) | copy-start | bytes 3145732
  0.0 2.3 %copy-start.1 = (bf16[16,1024]{1,0:T(8,128)(2,1)S(1)}, bf16[16,1024]{1,0:T(8,128)(2,1)}, u32[]{:S(2)}) copy-start(bf16[16,1024]{1,0:T(8,128)(2,1)} %param.9) | copy-start | bytes 98308
  2.3 9.1 %copy-start.2 = (s32[512]{0:T(512)S(1)}, s32[512]{0:T(512)}, u32[]{:S(2)}) copy-start(s32[512]{0:T(512)} %param.11) | copy-start | bytes 6148
  2.3 9.1 %copy-start.4 = (s32[128]{0:T(128)S(1)}, s32[128]{0:T(128)}, u32[]{:S(2)}) copy-start(s32[128]{0:T(128)} %param.10) | copy-start | bytes 1540
  2.3 15.8 %copy-start.5 = (bf16[512,512]{1,0:T(8,128)(2,1)S(1)}, bf16[512,512]{1,0:T(8,128)(2,1)}, u32[]{:S(2)}) copy-start(bf16[512,512]{1,0:T(8,128)(2,1)} %param.15) | copy-start | bytes 1572868
  2.3 15.8 %copy-start.6 = (bf16[512,512]{1,0:T(8,128)(2,1)S(1)}, bf16[512,512]{1,0:T(8,128)(2,1)}, u32[]{:S(2)}) copy-start(bf16[512,512]{1,0:T(8,128)(2,1)} %param.14) | copy-start | bytes 1572868
  3.4 14.6 %all-to-all-start = ((bf16[8,16,512]{2,1,0:T(8,128)(2,1)}), bf16[8,16,512]{2,1,0:T(8,128)(2,1)S(1)}, u32[]{:S(2)}, u32[]{:S(2)}) async-start(bf16[8,16,512]{2,1,0:T(8,128)(2,1)} %broadcast_in_dim.2), calls=%async_computation | async-start | bytes 262144 | tf_op jit(solution)/shard_map/all_to_all | solution.py:36
  18.1 13.1 %copy-start.3 = (f32[512]{0:T(512)S(1)}, f32[512]{0:T(512)}, u32[]{:S(2)}) copy-start(f32[512]{0:T(512)} %param.16) | copy-start | bytes 6148
  30.0 1.2 %collective-permute-start = (f32[2,16]{1,0:T(2,128)S(1)}, f32[2,16]{1,0:T(2,128)S(1)}, u32[]{:S(2)}, u32[]{:S(2)}) collective-permute-start(f32[2,16]{1,0:T(2,128)S(1)} %pad_maximum_fusion), channel_id=1, source_target_pairs={{0,1},{1,0},{2,3},{3,2},{4,5},{5,4},{6,7},{7,6},{8,9},{9,8},{10,11... | collective-permute-start | bytes 392 | tf_op jit(solution)/shard_map/ppermute | solution.py:17
  31.5 1.3 %collective-permute-start.1 = (f32[16,1024]{1,0:T(8,128)S(1)}, f32[16,1024]{1,0:T(8,128)S(1)}, u32[]{:S(2)}, u32[]{:S(2)}) collective-permute-start(f32[16,1024]{1,0:T(8,128)S(1)} %fusion.11), channel_id=1, source_target_pairs={{0,1},{1,0},{2,3},{3,2},{4,5},{5,4},{6,7},{7,6},{8,9},{9,8},{10,11... | collective-permute-start | bytes 196616 | tf_op jit(solution)/shard_map/ppermute | solution.py:17

commit v2 on v1

--- a/solution.py
+++ b/solution.py
@@ -51,8 +51,8 @@
         "hce,ehd->chd", attn_weights, value_heads, preferred_element_type=jnp.float32
     ).reshape(n_ev, row_count, local_width)
 
-    pieces = lax.all_to_all(partial_out, "events", 0, 0, tiled=False)
-    attended = jnp.sum(pieces, axis=0)
+    pieces = lax.all_to_all(partial_out.astype(jnp.bfloat16), "events", 0, 0, tiled=False)
+    attended = jnp.sum(pieces.astype(jnp.float32), axis=0)
 
     moments = jnp.stack([jnp.sum(attended, axis=1), jnp.sum(attended * attended, axis=1)])
     moments = partner_sum(moments)

time: 33.7 us -> 32.7 us (0.970)
  blocking collectives: 10.6 us -> 9.74 us
    all_to_all x1, blocking collectives: 10.6 us -> 9.74 us  [shards(): lax.all_to_all(partial_out.astype(jnp.bfloat16), 'events', 0, 0, tiled=Fa...]
where the time goes in v2:
time: 32.7 us; the launch traced here: 32.4 us
  blocking collectives  9.74 us (30%)
  waiting for transfers between devices  8.79 us (27%)
  starting transfers between devices  7.52 us (23%)
  local copies, waits for them, and re-layouts  3.15 us (10%)
  matrix products  1.34 us (4%)
  other arithmetic  1.03 us (3%)
  between operations  0.83 us (3%)
    all_to_all x1, blocking collectives, shards(): lax.all_to_all(partial_out.astype(jnp.bfloat16), 'events', 0, 0, tiled=Fa...  9.74 us
    all_to_all x1, starting transfers between devices, shards(): lax.all_to_all(spread, 'events', 0, 0, tiled=False)  7.28 us
    all_to_all x1, waiting for transfers between devices, shards(): lax.all_to_all(spread, 'events', 0, 0, tiled=False)  6.55 us
    unnamed x15, local copies, waits for them, and re-layouts  2.29 us
    ppermute x2, waiting for transfers between devices, partner_sum(): other = lax.ppermute(x, 'heads', [(i, (i + 1) % n) for i in range(n)])  2.24 us
  transfers between devices with their start and end apart: 3, of which 3 were waited for; matrix products, arithmetic and copies ran while one was open for 0% of the time, Pallas kernels for 0%

profile of v2, /device:TPU:0, one launch (start us, length us, event | category | flops | bytes accessed | tf_op | source)
XLA Modules:
  0.0 32.4 jit_solution(17313721674551394502)
XLA Ops:
  0.0 0.0 copy-start
  0.0 0.0 copy-start.1
  0.0 2.3 %copy.18 = bf16[128,8,2,512]{3,1,2,0:T(8,128)(2,1)S(1)} copy(bf16[128,8,2,512]{3,2,1,0:T(2,128)(2,1)} %bitcast.38) | data formatting | bytes 4194304
  2.3 0.0 copy-start.2
  2.3 0.0 copy-start.4
  2.3 0.0 copy-start.5
  2.3 0.0 copy-start.6
  2.3 0.0 copy-done.1
  2.3 0.4 %multiply_convert_fusion.1 = bf16[16,1024]{1,0:T(8,128)(2,1)S(1)} fusion(bf16[16,1024]{1,0:T(8,128)(2,1)S(1)} %copy-done.1, bf16[1024,1024]{1,0:T(8,128)(2,1)S(1)} %bitcast.37), kind=kOutput, calls=%fused_computation.16 | convolution fusion | flops 33636352 | bytes 2162688 | tf_op jit(solution)/shard_map/dot_general | solution.py:31
  2.8 0.7 %broadcast_in_dim.2 = bf16[8,16,512]{2,1,0:T(8,128)(2,1)} broadcast(bf16[16,512]{1,0:T(8,128)(2,1)S(1)} %slice.18), dimensions={1,2} | broadcast | bytes 147456 | tf_op jit(solution)/shard_map/broadcast_in_dim | solution.py:35
  3.4 7.3 %all-to-all-start = ((bf16[8,16,512]{2,1,0:T(8,128)(2,1)}), bf16[8,16,512]{2,1,0:T(8,128)(2,1)S(1)}, u32[]{:S(2)}, u32[]{:S(2)}) async-start(bf16[8,16,512]{2,1,0:T(8,128)(2,1)} %broadcast_in_dim.2), calls=%async_computation | async-start | bytes 262144 | tf_op jit(solution)/shard_map/all_to_all | solution.py:36
  11.3 0.0 copy-done.2
  11.4 0.0 copy-done.4
  11.4 0.1 and_convert_fusion
  11.5 6.5 %all-to-all-done = bf16[8,16,512]{2,1,0:T(8,128)(2,1)S(1)} async-done(((bf16[8,16,512]{2,1,0:T(8,128)(2,1)}), bf16[8,16,512]{2,1,0:T(8,128)(2,1)S(1)}, u32[]{:S(2)}, u32[]{:S(2)}) %all-to-all-start) | async-done | bytes 131104 | tf_op jit(solution)/shard_map/all_to_all | solution.py:36
  18.1 0.0 copy-done.5
  18.1 0.0 copy-done.6
  18.1 0.0 copy-start.3
  18.1 0.6 %fusion = bf16[128,4,128]{2,0,1:T(8,128)(2,1)S(1)} fusion(f32[128,512]{1,0:T(8,128)S(1)} %and_convert_fusion, bf16[128,4,128]{2,1,0:T(4,128)(2,1)S(1)} %reshape_reshape.3, bf16[512,512]{1,0:T(8,128)(2,1)S(1)} %copy-done.5, bf16[512,512]{1,0:T(8,128)(2,1)S(1)} %copy-done.6), kind=kOutput, calls=%fused_computation.2 | convolution fusion | flops 136118272 | bytes 1572864 | tf_op jit(solution)/shard_map/hce,ehd->chd/dot_general | solution.py:50
  18.7 0.1 copy.15
  18.9 0.1 convert_element_type.41
  18.9 9.7 %all_to_all.10 = bf16[8,16,512]{2,1,0:T(8,128)(2,1)S(1)} all-to-all(bf16[8,16,512]{2,1,0:T(8,128)(2,1)S(1)} %convert_element_type.41), channel_id=1, replica_groups=mesh['groups'=2,'events'=8,'heads'=2] {'events'}, dimensions={0} | all-to-all | bytes 262144 | tf_op jit(solution)/shard_map/all_to_all | solution.py:54
  28.7 0.1 convert_reduce_fusion
  28.8 0.1 multiply_reduce_fusion
  28.9 0.1 collective-permute-start
  29.0 1.1 %collective-permute-done = f32[2,16]{1,0:T(2,128)S(1)} collective-permute-done((f32[2,16]{1,0:T(2,128)S(1)}, f32[2,16]{1,0:T(2,128)S(1)}, u32[]{:S(2)}, u32[]{:S(2)}) %collective-permute-start) | collective-permute-done | bytes 160 | tf_op jit(solution)/shard_map/ppermute | solution.py:17
  30.2 0.0 copy-done
  30.2 0.0 copy-done.3
  30.2 0.3 fusion.12
  30.5 0.2 collective-permute-start.1
  30.7 1.1 %collective-permute-done.1 = f32[16,1024]{1,0:T(8,128)S(1)} collective-permute-done((f32[16,1024]{1,0:T(8,128)S(1)}, f32[16,1024]{1,0:T(8,128)S(1)}, u32[]{:S(2)}, u32[]{:S(2)}) %collective-permute-start.1) | collective-permute-done | bytes 65568 | tf_op jit(solution)/shard_map/ppermute | solution.py:17
  31.8 0.6 %add_convert_fusion = bf16[16,1024]{1,0:T(8,128)(2,1)} fusion(f32[16,1024]{1,0:T(8,128)S(1)} %fusion.12, f32[16,1024]{1,0:T(8,128)S(1)} %collective-permute-done.1, bf16[16,1024]{1,0:T(8,128)(2,1)S(1)} %copy-done.1), kind=kLoop, calls=%fused_computation.15 | loop fusion | flops 65536 | bytes 196608 | tf_op jit(solution)/shard_map/convert_element_type | solution.py:65
  (7 shorter events, 0.1 us)
Async XLA Ops:
  0.0 30.2 %copy-start = (bf16[512,1024]{1,0:T(8,128)(2,1)S(1)}, bf16[512,1024]{1,0:T(8,128)(2,1)}, u32[]{:S(2)}) copy-start(bf16[512,1024]{1,0:T(8,128)(2,1)} %param.17) | copy-start | bytes 3145732
  0.0 2.3 %copy-start.1 = (bf16[16,1024]{1,0:T(8,128)(2,1)S(1)}, bf16[16,1024]{1,0:T(8,128)(2,1)}, u32[]{:S(2)}) copy-start(bf16[16,1024]{1,0:T(8,128)(2,1)} %param.9) | copy-start | bytes 98308
  2.3 9.1 %copy-start.2 = (s32[512]{0:T(512)S(1)}, s32[512]{0:T(512)}, u32[]{:S(2)}) copy-start(s32[512]{0:T(512)} %param.11) | copy-start | bytes 6148
  2.3 9.1 %copy-start.4 = (s32[128]{0:T(128)S(1)}, s32[128]{0:T(128)}, u32[]{:S(2)}) copy-start(s32[128]{0:T(128)} %param.10) | copy-start | bytes 1540
  2.3 15.8 %copy-start.5 = (bf16[512,512]{1,0:T(8,128)(2,1)S(1)}, bf16[512,512]{1,0:T(8,128)(2,1)}, u32[]{:S(2)}) copy-start(bf16[512,512]{1,0:T(8,128)(2,1)} %param.15) | copy-start | bytes 1572868
  2.3 15.8 %copy-start.6 = (bf16[512,512]{1,0:T(8,128)(2,1)S(1)}, bf16[512,512]{1,0:T(8,128)(2,1)}, u32[]{:S(2)}) copy-start(bf16[512,512]{1,0:T(8,128)(2,1)} %param.14) | copy-start | bytes 1572868
  3.4 14.6 %all-to-all-start = ((bf16[8,16,512]{2,1,0:T(8,128)(2,1)}), bf16[8,16,512]{2,1,0:T(8,128)(2,1)S(1)}, u32[]{:S(2)}, u32[]{:S(2)}) async-start(bf16[8,16,512]{2,1,0:T(8,128)(2,1)} %broadcast_in_dim.2), calls=%async_computation | async-start | bytes 262144 | tf_op jit(solution)/shard_map/all_to_all | solution.py:36
  18.1 12.1 %copy-start.3 = (f32[512]{0:T(512)S(1)}, f32[512]{0:T(512)}, u32[]{:S(2)}) copy-start(f32[512]{0:T(512)} %param.16) | copy-start | bytes 6148
  28.9 1.2 %collective-permute-start = (f32[2,16]{1,0:T(2,128)S(1)}, f32[2,16]{1,0:T(2,128)S(1)}, u32[]{:S(2)}, u32[]{:S(2)}) collective-permute-start(f32[2,16]{1,0:T(2,128)S(1)} %pad_maximum_fusion), channel_id=1, source_target_pairs={{0,1},{1,0},{2,3},{3,2},{4,5},{5,4},{6,7},{7,6},{8,9},{9,8},{10,11... | collective-permute-start | bytes 392 | tf_op jit(solution)/shard_map/ppermute | solution.py:17
  30.5 1.3 %collective-permute-start.1 = (f32[16,1024]{1,0:T(8,128)S(1)}, f32[16,1024]{1,0:T(8,128)S(1)}, u32[]{:S(2)}, u32[]{:S(2)}) collective-permute-start(f32[16,1024]{1,0:T(8,128)S(1)} %fusion.12), channel_id=1, source_target_pairs={{0,1},{1,0},{2,3},{3,2},{4,5},{5,4},{6,7},{7,6},{8,9},{9,8},{10,11... | collective-permute-start | bytes 196616 | tf_op jit(solution)/shard_map/ppermute | solution.py:17

commit v3 on v2

--- a/solution.py
+++ b/solution.py
@@ -12,10 +12,9 @@
 epsilon = 1e-05
 
 
-def partner_sum(x):
+def swap(x):
     n = lax.axis_size("heads")
-    other = lax.ppermute(x, "heads", [(i, (i + 1) % n) for i in range(n)])
-    return x + other
+    return lax.ppermute(x, "heads", [(i, (i + 1) % n) for i in range(n)])
 
 
 def shards(inputs, cand_user, event_user, event_count, w_qu, keys, values, gain, w_out):
@@ -54,14 +53,27 @@
     pieces = lax.all_to_all(partial_out.astype(jnp.bfloat16), "events", 0, 0, tiled=False)
     attended = jnp.sum(pieces.astype(jnp.float32), axis=0)
 
-    moments = jnp.stack([jnp.sum(attended, axis=1), jnp.sum(attended * attended, axis=1)])
-    moments = partner_sum(moments)
-    average = moments[0] / HD
-    variance = moments[1] / HD - average * average
-    normed = (attended - average[:, None]) * lax.rsqrt(variance + epsilon)[:, None] * gain
-    gated = (normed * gate_values.astype(jnp.float32)).astype(jnp.bfloat16)
-    projected = jnp.dot(gated, w_out, preferred_element_type=jnp.float32)
-    summed_heads = partner_sum(projected)
+    first = jnp.sum(attended, axis=1)
+    second = jnp.sum(attended * attended, axis=1)
+    weighting = gain * gate_values.astype(jnp.float32)
+    centred = (attended - (first / local_width)[:, None]) * weighting
+    lhs = jnp.concatenate([centred, weighting], axis=0).astype(jnp.bfloat16)
+    terms = jnp.dot(lhs, w_out, preferred_element_type=jnp.float32)
+    packet = jnp.concatenate([terms.reshape(-1), first, second])
+    other = swap(packet)
+    cut = terms.size
+    terms_other = other[:cut].reshape(terms.shape)
+    first_other = other[cut:cut + row_count]
+    second_other = other[cut + row_count:]
+
+    average = (first + first_other) / HD
+    variance = (second + second_other) / HD - average * average
+    scale = lax.rsqrt(variance + epsilon)
+    centred_sum = terms[:row_count] + terms_other[:row_count]
+    shift = (average - first / local_width)[:, None] * terms[row_count:] + (
+        average - first_other / local_width
+    )[:, None] * terms_other[row_count:]
+    summed_heads = scale[:, None] * (centred_sum - shift)
     return (inputs.astype(jnp.float32) + summed_heads).astype(jnp.bfloat16)
 
 

time: 32.7 us -> 31.9 us (0.976)
  waiting for transfers between devices: 8.79 us -> 7.89 us
    ppermute x2 -> x1, waiting for transfers between devices: 2.24 us -> 1.34 us  [swap(): return lax.ppermute(x, 'heads', [(i, (i + 1) % n) for i in range(n)])]
    unnamed x15 -> x16, local copies, waits for them, and re-layouts: 2.29 us -> 2.32 us
  transfers between devices with their start and end apart: 3 -> 2, of which waited for: 3 -> 2; matrix products, arithmetic and copies ran while one was open for 0% -> 0% of each run, Pallas kernels for 0% -> 0%
where the time goes in v3:
time: 31.9 us; the launch traced here: 31.6 us
  blocking collectives  9.74 us (31%)
  waiting for transfers between devices  7.89 us (25%)
  starting transfers between devices  7.29 us (23%)
  local copies, waits for them, and re-layouts  3.31 us (10%)
  matrix products  1.33 us (4%)
  other arithmetic  1.17 us (4%)
  between operations  0.83 us (3%)
    all_to_all x1, blocking collectives, shards(): lax.all_to_all(partial_out.astype(jnp.bfloat16), 'events', 0, 0, tiled=Fa...  9.74 us
    all_to_all x1, starting transfers between devices, shards(): lax.all_to_all(spread, 'events', 0, 0, tiled=False)  7.28 us
    all_to_all x1, waiting for transfers between devices, shards(): lax.all_to_all(spread, 'events', 0, 0, tiled=False)  6.55 us
    unnamed x16, local copies, waits for them, and re-layouts  2.32 us
    ppermute x1, waiting for transfers between devices, swap(): return lax.ppermute(x, 'heads', [(i, (i + 1) % n) for i in range(n)])  1.34 us
    convert_element_type x1, other arithmetic, shards(): return (inputs.astype(jnp.float32) + summed_heads).astype(jnp.bfloat16)  0.71 us
    broadcast_in_dim x1, local copies, waits for them, and re-layouts, shards(): spread = jnp.broadcast_to(query_local[None], (n_ev, row_count, local_width))  0.65 us
    dot_general x1, matrix products, shards(): jnp.einsum('hce,ehd->chd', attn_weights, value_heads, preferred_element_t...  0.65 us
  transfers between devices with their start and end apart: 2, of which 2 were waited for; matrix products, arithmetic and copies ran while one was open for 0% of the time, Pallas kernels for 0%

profile of v3, /device:TPU:0, one launch (start us, length us, event | category | flops | bytes accessed | tf_op | source)
XLA Modules:
  0.0 31.6 jit_solution(17181618652339372036)
XLA Ops:
  0.0 0.0 copy-start
  0.0 0.0 copy-start.1
  0.0 2.3 %copy.18 = bf16[128,8,2,512]{3,1,2,0:T(8,128)(2,1)S(1)} copy(bf16[128,8,2,512]{3,2,1,0:T(2,128)(2,1)} %bitcast.28) | data formatting | bytes 4194304
  2.3 0.0 copy-start.2
  2.3 0.0 copy-start.4
  2.3 0.0 copy-start.5
  2.3 0.0 copy-start.6
  2.3 0.0 copy-done.1
  2.3 0.4 %multiply_convert_fusion.1 = bf16[16,1024]{1,0:T(8,128)(2,1)S(1)} fusion(bf16[16,1024]{1,0:T(8,128)(2,1)S(1)} %copy-done.1, bf16[1024,1024]{1,0:T(8,128)(2,1)S(1)} %bitcast.27), kind=kOutput, calls=%fused_computation.22 | convolution fusion | flops 33636352 | bytes 2162688 | tf_op jit(solution)/shard_map/dot_general | solution.py:30
  2.7 0.7 %broadcast_in_dim.2 = bf16[8,16,512]{2,1,0:T(8,128)(2,1)} broadcast(bf16[16,512]{1,0:T(8,128)(2,1)S(1)} %slice.49), dimensions={1,2} | broadcast | bytes 147456 | tf_op jit(solution)/shard_map/broadcast_in_dim | solution.py:34
  3.4 7.3 %all-to-all-start = ((bf16[8,16,512]{2,1,0:T(8,128)(2,1)}), bf16[8,16,512]{2,1,0:T(8,128)(2,1)S(1)}, u32[]{:S(2)}, u32[]{:S(2)}) async-start(bf16[8,16,512]{2,1,0:T(8,128)(2,1)} %broadcast_in_dim.2), calls=%async_computation | async-start | bytes 262144 | tf_op jit(solution)/shard_map/all_to_all | solution.py:35
  11.3 0.0 copy-done.2
  11.4 0.0 copy-done.4
  11.4 0.1 and_convert_fusion
  11.5 6.5 %all-to-all-done = bf16[8,16,512]{2,1,0:T(8,128)(2,1)S(1)} async-done(((bf16[8,16,512]{2,1,0:T(8,128)(2,1)}), bf16[8,16,512]{2,1,0:T(8,128)(2,1)S(1)}, u32[]{:S(2)}, u32[]{:S(2)}) %all-to-all-start) | async-done | bytes 131104 | tf_op jit(solution)/shard_map/all_to_all | solution.py:35
  18.1 0.0 copy-done.5
  18.1 0.0 copy-done.6
  18.1 0.0 copy-start.3
  18.1 0.6 %fusion = bf16[128,4,128]{2,0,1:T(8,128)(2,1)S(1)} fusion(f32[128,512]{1,0:T(8,128)S(1)} %and_convert_fusion, bf16[128,4,128]{2,1,0:T(4,128)(2,1)S(1)} %reshape_reshape.3, bf16[512,512]{1,0:T(8,128)(2,1)S(1)} %copy-done.5, bf16[512,512]{1,0:T(8,128)(2,1)S(1)} %copy-done.6), kind=kOutput, calls=%fused_computation.2 | convolution fusion | flops 136118272 | bytes 1572864 | tf_op jit(solution)/shard_map/hce,ehd->chd/dot_general | solution.py:49
  18.7 0.1 copy.15
  18.9 0.1 convert_element_type.39
  18.9 9.7 %all_to_all.10 = bf16[8,16,512]{2,1,0:T(8,128)(2,1)S(1)} all-to-all(bf16[8,16,512]{2,1,0:T(8,128)(2,1)S(1)} %convert_element_type.39), channel_id=1, replica_groups=mesh['groups'=2,'events'=8,'heads'=2] {'events'}, dimensions={0} | all-to-all | bytes 262144 | tf_op jit(solution)/shard_map/all_to_all | solution.py:53
  28.7 0.1 convert_reduce_fusion
  28.8 0.0 copy-done.3
  28.8 0.1 multiply_convert_fusion.2
  28.9 0.0 copy-done
  28.9 0.3 fusion.17
  29.3 0.1 concatenate.8
  29.4 0.0 collective-permute-start
  29.4 1.3 %collective-permute-done = f32[32800]{0:T(1024)S(1)} collective-permute-done((f32[32800]{0:T(1024)S(1)}, f32[32800]{0:T(1024)S(1)}, u32[]{:S(2)}, u32[]{:S(2)}) %collective-permute-start) | collective-permute-done | bytes 131232 | tf_op jit(solution)/shard_map/ppermute | solution.py:17
  30.8 0.1 add_rsqrt_fusion
  30.8 0.7 %fusion.16 = bf16[16,1024]{1,0:T(8,128)(2,1)} fusion(f32[32,1024]{1,0:T(8,128)S(1)} %fusion.17, f32[16,1024]{1,0:T(8,128)S(1)} %slice.45, f32[16,1024]{1,0:T(8,128)S(1)} %slice.48, bf16[16,1024]{1,0:T(8,128)(2,1)S(1)} %copy-done.1, f32[16]{0:T(128)S(1)} %get-tuple-element.8, f32[16]{0:T(128)S(1)} %get-tuple-element.9, f32[16]{0:T(128)S(1)} %get-tuple-element.7), kind=kLoop, calls=%fused_computation.20 | loop fusion | flops 147456 | bytes 327872 | tf_op jit(solution)/shard_map/convert_element_type | solution.py:77
  (8 shorter events, 0.1 us)
Async XLA Ops:
  0.0 28.9 %copy-start = (bf16[512,1024]{1,0:T(8,128)(2,1)S(1)}, bf16[512,1024]{1,0:T(8,128)(2,1)}, u32[]{:S(2)}) copy-start(bf16[512,1024]{1,0:T(8,128)(2,1)} %param.17) | copy-start | bytes 3145732
  0.0 2.3 %copy-start.1 = (bf16[16,1024]{1,0:T(8,128)(2,1)S(1)}, bf16[16,1024]{1,0:T(8,128)(2,1)}, u32[]{:S(2)}) copy-start(bf16[16,1024]{1,0:T(8,128)(2,1)} %param.9) | copy-start | bytes 98308
  2.3 9.1 %copy-start.2 = (s32[512]{0:T(512)S(1)}, s32[512]{0:T(512)}, u32[]{:S(2)}) copy-start(s32[512]{0:T(512)} %param.11) | copy-start | bytes 6148
  2.3 9.1 %copy-start.4 = (s32[128]{0:T(128)S(1)}, s32[128]{0:T(128)}, u32[]{:S(2)}) copy-start(s32[128]{0:T(128)} %param.10) | copy-start | bytes 1540
  2.3 15.8 %copy-start.5 = (bf16[512,512]{1,0:T(8,128)(2,1)S(1)}, bf16[512,512]{1,0:T(8,128)(2,1)}, u32[]{:S(2)}) copy-start(bf16[512,512]{1,0:T(8,128)(2,1)} %param.15) | copy-start | bytes 1572868
  2.3 15.8 %copy-start.6 = (bf16[512,512]{1,0:T(8,128)(2,1)S(1)}, bf16[512,512]{1,0:T(8,128)(2,1)}, u32[]{:S(2)}) copy-start(bf16[512,512]{1,0:T(8,128)(2,1)} %param.14) | copy-start | bytes 1572868
  3.4 14.6 %all-to-all-start = ((bf16[8,16,512]{2,1,0:T(8,128)(2,1)}), bf16[8,16,512]{2,1,0:T(8,128)(2,1)S(1)}, u32[]{:S(2)}, u32[]{:S(2)}) async-start(bf16[8,16,512]{2,1,0:T(8,128)(2,1)} %broadcast_in_dim.2), calls=%async_computation | async-start | bytes 262144 | tf_op jit(solution)/shard_map/all_to_all | solution.py:35
  18.1 10.7 %copy-start.3 = (f32[512]{0:T(512)S(1)}, f32[512]{0:T(512)}, u32[]{:S(2)}) copy-start(f32[512]{0:T(512)} %param.16) | copy-start | bytes 6148
  29.4 1.4 %collective-permute-start = (f32[32800]{0:T(1024)S(1)}, f32[32800]{0:T(1024)S(1)}, u32[]{:S(2)}, u32[]{:S(2)}) collective-permute-start(f32[32800]{0:T(1024)S(1)} %concatenate.8), channel_id=1, source_target_pairs={{0,1},{1,0},{2,3},{3,2},{4,5},{5,4},{6,7},{7,6},{8,9},{9,8},{10,11... | collective-permute-start | bytes 393608 | tf_op jit(solution)/shard_map/ppermute | solution.py:17
